TPU v7x, 128 devices: a whole 4x4x4 slice. The times are simulated.
128 devices in a mesh: rep: 4 (over z), shard: 32 (over x, y, core).
Axes of the slice: x: 4, y: 4, z: 4, core: 2. Of those that a mesh axis runs over, the one named last changes fastest.
Arguments:
- trained_sq: float32 [4, 4, 768, 768], P('rep', None, 'shard'), may hold values from -6 to 6
- trained_up: float32 [4, 768, 3072], P('rep', 'shard'), may hold values from -6 to 6
- trained_down: float32 [4, 3072, 768], P('rep', 'shard'), may hold values from -6 to 6
- trained_ln: float32 [4, 4, 768], P('rep', None, 'shard'), may hold values from -6 to 6
- start_sq: float32 [4, 768, 768], P(None, 'shard'), may hold values from -6 to 6
- start_up: float32 [768, 3072], P('shard'), may hold values from -6 to 6
- start_down: float32 [3072, 768], P('shard'), may hold values from -6 to 6
- start_ln: float32 [4, 768], P(None, 'shard'), may hold values from -6 to 6
- resid_sq: float32 [4, 4, 768, 768], P('rep', None, 'shard'), may hold values from -4 to 4
- resid_up: float32 [4, 768, 3072], P('rep', 'shard'), may hold values from -4 to 4
- resid_down: float32 [4, 3072, 768], P('rep', 'shard'), may hold values from -4 to 4
- mom_sq: float32 [4, 768, 768], P(None, 'shard'), may hold values from -3 to 3
- mom_up: float32 [768, 3072], P('shard'), may hold values from -3 to 3
- mom_down: float32 [3072, 768], P('shard'), may hold values from -3 to 3
- mom_ln: float32 [4, 768], P(None, 'shard'), may hold values from -3 to 3
- basis_sq: float32 [4, 768, 64], replicated, may hold values from -0.21875 to 0.21875
- basis_up: float32 [3072, 64], replicated, may hold values from -0.109375 to 0.109375
- basis_down: float32 [768, 64], replicated, may hold values from -0.21875 to 0.21875
Outputs:
- new_resid_sq: float32 [4, 4, 768, 768], P('rep', None, 'shard')
- new_resid_up: float32 [4, 768, 3072], P('rep', 'shard')
- new_resid_down: float32 [4, 3072, 768], P('rep', 'shard')
- new_mom_sq: float32 [4, 768, 768], P(None, 'shard')
- new_mom_up: float32 [768, 3072], P('shard')
- new_mom_down: float32 [3072, 768], P('shard')
- new_mom_ln: float32 [4, 768], P(None, 'shard')
- weights_sq: bfloat16 [4, 768, 768], replicated
- weights_up: bfloat16 [768, 3072], replicated
- weights_down: bfloat16 [3072, 768], replicated
- weights_ln: bfloat16 [4, 768], replicated
All inputs are finite; a program needn't handle non-finite values.
Results may differ from a plain program's by a relative error of at most 0.001.
Values may be sent and summed in bfloat16 or wider, within the bound.
No kernel may reach another device: no remote copies, remote signals or barrier semaphores. Data moves between devices by JAX's collectives and lax.ppermute only.
A program may use at most 128 MiB of HBM per device.

v0:
```python
import jax
import jax.numpy as jnp
from jax import lax
from jax.sharding import PartitionSpec as P

moment_coef = 0.9
outer_rate = 0.7


def advance(start, moment, outer):
    new_moment = moment_coef * moment + outer
    weights = (start - outer_rate * (outer + moment_coef * new_moment)).astype(jnp.bfloat16)
    return (new_moment, weights)


def on_device(
    trained_sq,
    trained_up,
    trained_down,
    trained_ln,
    start_sq,
    start_up,
    start_down,
    start_ln,
    resid_sq,
    resid_up,
    resid_down,
    mom_sq,
    mom_up,
    mom_down,
    mom_ln,
    basis_sq,
    basis_up,
    basis_down,
):
    highest = lax.Precision.HIGHEST
    groups = lax.axis_size("rep")
    delta_sq = start_sq - trained_sq[0] + resid_sq[0]
    factor_sq = jnp.einsum("mrd,mdk->mrk", delta_sq, basis_sq, precision=highest)
    new_resid_sq = delta_sq - jnp.einsum("mrk,mdk->mrd", factor_sq, basis_sq, precision=highest)
    delta_up = start_up - trained_up[0] + resid_up[0]
    factor_up = jnp.dot(delta_up, basis_up, precision=highest, preferred_element_type=jnp.float32)
    new_resid_up = delta_up - jnp.einsum("rk,fk->rf", factor_up, basis_up, precision=highest)
    delta_down = start_down - trained_down[0] + resid_down[0]
    factor_down = jnp.dot(
        delta_down, basis_down, precision=highest, preferred_element_type=jnp.float32
    )
    new_resid_down = delta_down - jnp.einsum(
        "rk,dk->rd", factor_down, basis_down, precision=highest
    )
    norm_delta = start_ln - trained_ln[0]
    summed = lax.psum((factor_sq, factor_up, factor_down, norm_delta), "rep")
    mean_sq = summed[0] / groups
    mean_up = summed[1] / groups
    mean_down = summed[2] / groups
    mean_ln = summed[3] / groups
    new_mom_ln, norm_weights = advance(start_ln, mom_ln, mean_ln)
    outer_sq = jnp.einsum("mrk,mdk->mrd", mean_sq, basis_sq, precision=highest)
    outer_up = jnp.einsum("rk,fk->rf", mean_up, basis_up, precision=highest)
    outer_down = jnp.einsum("rk,dk->rd", mean_down, basis_down, precision=highest)
    new_mom_sq, owned_sq = advance(start_sq, mom_sq, outer_sq)
    new_mom_up, owned_up = advance(start_up, mom_up, outer_up)
    new_mom_down, owned_down = advance(start_down, mom_down, outer_down)
    weights_sq, weights_up, weights_down, weights_ln = (
        lax.all_gather(owned_sq, "shard", axis=1, tiled=True),
        lax.all_gather(owned_up, "shard", axis=0, tiled=True),
        lax.all_gather(owned_down, "shard", axis=0, tiled=True),
        lax.all_gather(norm_weights, "shard", axis=1, tiled=True),
    )
    return (
        new_resid_sq[None],
        new_resid_up[None],
        new_resid_down[None],
        new_mom_sq,
        new_mom_up,
        new_mom_down,
        new_mom_ln,
        weights_sq,
        weights_up,
        weights_down,
        weights_ln,
    )


def solution(mesh):
    placed = (
        P("rep", None, "shard", None),
        P("rep", "shard", None),
        P("rep", "shard", None),
        P("rep", None, "shard"),
        P(None, "shard", None),
        P("shard", None),
        P("shard", None),
        P(None, "shard"),
        P("rep", None, "shard", None),
        P("rep", "shard", None),
        P("rep", "shard", None),
        P(None, "shard", None),
        P("shard", None),
        P("shard", None),
        P(None, "shard"),
        P(),
        P(),
        P(),
    )
    return jax.shard_map(
        on_device,
        mesh=mesh,
        in_specs=placed,
        out_specs=(
            P("rep", None, "shard", None),
            P("rep", "shard", None),
            P("rep", "shard", None),
            P(None, "shard", None),
            P("shard", None),
            P("shard", None),
            P(None, "shard"),
            P(),
            P(),
            P(),
            P(),
        ),
        check_vma=False,
    )
```

profile of v0, /device:TPU:1, one launch (start us, length us, event | category | flops | bytes accessed | tf_op | source)
XLA Modules:
  0.0 201.4 jit_solution(2891028444277751555)
XLA Ops:
  7.3 0.9 bitcast_subtract_fusion.3
  8.2 0.5 copy-done
  8.7 2.6 %fusion.16 = f32[4,24,64]{2,1,0:T(8,128)} fusion(f32[4,768,64]{1,2,0:T(8,128)S(1)} %copy-done, f32[1,4,24,768]{3,2,1,0:T(8,128)} %param.26, f32[4,24,768]{2,1,0:T(8,128)} %param.22, f32[1,4,24,768]{3,2,1,0:T(8,128)} %param.18), kind=kOutput, calls=%fused_computation.34 | convolution fusion | flops 56770560 | bytes 1695744 | tf_op jit(solution)/shard_map/mrd,mdk->mrk/dot_general | solution.py:39
  11.2 2.3 %fusion.18 = f32[96,64]{0,1:T(8,128)} fusion(f32[768,64]{0,1:T(8,128)} %param.35, f32[1,96,768]{2,1,0:T(8,128)} %param.28, f32[96,768]{1,0:T(8,128)} %param.24, f32[1,96,768]{2,1,0:T(8,128)} %param.20), kind=kOutput, calls=%fused_computation.36 | convolution fusion | flops 56770560 | bytes 1105920 | tf_op jit(solution)/shard_map/dot_general | solution.py:45
  13.5 2.1 %fusion.17 = f32[24,64]{1,0:T(8,128)S(1)} fusion(f32[3072,64]{0,1:T(8,128)} %param.34, f32[1,24,3072]{2,1,0:T(8,128)} %param.27, f32[24,3072]{1,0:T(8,128)} %param.23, f32[1,24,3072]{2,1,0:T(8,128)} %param.19), kind=kOutput, calls=%fused_computation.35 | convolution fusion | flops 56770560 | bytes 1677312 | tf_op jit(solution)/shard_map/dot_general | solution.py:42
  15.6 17.3 %all-reduce = (f32[4,24,64]{2,1,0:T(8,128)}, f32[24,64]{1,0:T(8,128)}, f32[96,64]{0,1:T(8,128)}, f32[4,24]{1,0:T(4,128)}) all-reduce(f32[4,24,64]{2,1,0:T(8,128)} %fusion.16, f32[24,64]{1,0:T(8,128)S(1)} %fusion.17, f32[96,64]{0,1:T(8,128)} %fusion.18, f32[4,24]{1,0:T(4,128)S(1)} %bitcast_subtract_fusion.3), channel_id=1, replica_groups=mesh['rep'=4,'shard'=32] {'rep'}, use_global_device_ids=true, to_apply=%region_0.0 | all-reduce | flops 13920 | bytes 111360 | tf_op jit(solution)/shard_map/psum | solution.py:52
  33.0 2.3 %subtract_convert_fusion.2 = (bf16[4,24,768]{2,1,0:T(8,128)(2,1)}, f32[4,24,768]{2,1,0:T(8,128)}) fusion(f32[4,24,768]{2,1,0:T(8,128)S(1)} %copy-done.5, f32[4,24,768]{2,1,0:T(8,128)} %param.29, f32[4,768,64]{1,2,0:T(8,128)S(1)} %copy-done, f32[4,24,64]{2,1,0:T(8,128)} %get-tuple-element.11), kind=kOutput, calls=%fused_computation.14 | convolution fusion | flops 57145344 | bytes 1843200 | tf_op jit(solution)/shard_map/mrk,mdk->mrd/dot_general | solution.py:58
  35.4 2.3 %subtract_convert_fusion.1 = (bf16[24,3072]{1,0:T(8,128)(2,1)}, f32[24,3072]{1,0:T(8,128)}) fusion(f32[24,3072]{1,0:T(8,128)S(1)} %copy-done.3, f32[24,3072]{1,0:T(8,128)} %param.30, f32[3072,64]{0,1:T(8,128)S(1)} %copy-done.1, f32[24,64]{1,0:T(8,128)} %get-tuple-element.12), kind=kOutput, calls=%fused_computation.13 | convolution fusion | flops 57140736 | bytes 1824768 | tf_op jit(solution)/shard_map/rk,fk->rf/dot_general | solution.py:59
  37.7 2.2 %subtract_convert_fusion = (bf16[96,768]{1,0:T(8,128)(2,1)}, f32[96,768]{1,0:T(8,128)}) fusion(f32[96,768]{1,0:T(8,128)S(1)} %copy-done.4, f32[96,768]{1,0:T(8,128)} %param.31, f32[768,64]{0,1:T(8,128)S(1)} %copy-done.6, f32[96,64]{0,1:T(8,128)} %get-tuple-element.13), kind=kOutput, calls=%fused_computation.12 | convolution fusion | flops 57145344 | bytes 1253376 | tf_op jit(solution)/shard_map/rk,dk->rd/dot_general | solution.py:60
  40.0 1.3 fusion.12
  41.3 28.7 %all-gather = bf16[32,24,4]{1,2,0:T(4,128)(2,1)S(1)} all-gather(bf16[1,24,4]{1,2,0:T(4,128)(2,1)S(1)} %get-tuple-element.15), channel_id=1, replica_groups=mesh['rep'=4,'shard'=32] {'shard'}, dimensions={0}, use_global_device_ids=true | all-gather | bytes 6336 | tf_op jit(solution)/shard_map/all_gather | solution.py:68
  69.9 0.6 copy.30
  70.6 1.5 reshape.23
  72.0 2.1 %fusion.1 = f32[1,96,768]{2,1,0:T(8,128)} fusion(f32[96,64]{0,1:T(8,128)} %fusion.18, f32[768,64]{0,1:T(8,128)S(1)} %copy-done.6, f32[1,96,768]{2,1,0:T(8,128)S(1)} %copy-done.9, f32[96,768]{1,0:T(8,128)S(1)} %copy-done.4, f32[1,96,768]{2,1,0:T(8,128)} %param.20), kind=kOutput, calls=%fused_computation.3 | convolution fusion | flops 56844288 | bytes 1400832 | tf_op jit(solution)/shard_map/rk,dk->rd/dot_general | solution.py:48
  74.2 1.2 fusion
  75.4 2.3 %fusion.2 = f32[1,4,24,768]{3,2,1,0:T(8,128)} fusion(f32[4,24,64]{2,1,0:T(8,128)} %fusion.16, f32[4,768,64]{1,2,0:T(8,128)S(1)} %copy-done, f32[1,4,24,768]{3,2,1,0:T(8,128)} %param.26, f32[4,24,768]{2,1,0:T(8,128)S(1)} %copy-done.5, f32[1,4,24,768]{3,2,1,0:T(8,128)} %param.18), kind=kOutput, calls=%fused_computation.5 | convolution fusion | flops 56844288 | bytes 1990656 | tf_op jit(solution)/shard_map/mrk,mdk->mrd/dot_general | solution.py:40
  77.7 8.5 %all-gather.5.cloned.1.call-done = bf16[4,768,768]{2,1,0:T(8,128)(2,1)} async-done(((bf16[4,24,768]{2,1,0:T(8,128)(2,1)}), bf16[4,768,768]{2,1,0:T(8,128)(2,1)}) %all-gather.5.cloned.1.call-update) | async-done | bytes 4718608 | tf_op jit(solution)/shard_map/all_gather | solution.py:65
  86.2 49.0 %all-gather.7.cloned.1.call-done = bf16[768,3072]{1,0:T(8,128)(2,1)} async-done(((bf16[24,3072]{1,0:T(8,128)(2,1)}), bf16[768,3072]{1,0:T(8,128)(2,1)}) %all-gather.7.cloned.1.call-update) | async-done | bytes 4718608 | tf_op jit(solution)/shard_map/all_gather | solution.py:66
  135.1 49.0 %all-gather.9.cloned.1.call-done = bf16[3072,768]{1,0:T(8,128)(2,1)} async-done(((bf16[96,768]{1,0:T(8,128)(2,1)}), bf16[3072,768]{1,0:T(8,128)(2,1)}) %all-gather.9.cloned.1.call-update) | async-done | bytes 4718608 | tf_op jit(solution)/shard_map/all_gather | solution.py:67
  184.1 5.2 %copy.34 = bf16[4,768,768]{2,1,0:T(8,128)(2,1)} copy(bf16[4,768,768]{2,1,0:T(8,128)(2,1)} %all-gather.5.cloned.1.call-done) | data formatting | bytes 9437184
  189.3 2.4 %copy.35 = bf16[768,3072]{1,0:T(8,128)(2,1)} copy(bf16[768,3072]{1,0:T(8,128)(2,1)S(1)} %copy-done.2) | data formatting | bytes 9437184
  191.7 0.5 slice-done
  192.2 0.5 slice-done.1
  192.7 2.2 %copy.36 = bf16[3072,768]{1,0:T(8,128)(2,1)} copy(bf16[3072,768]{1,0:T(8,128)(2,1)S(1)} %bitcast.64) | data formatting | bytes 9437184
  (30 shorter events, 0.2 us)
Async XLA Ops:
  7.2 1.5 copy-start
  7.2 25.8 %copy-start.5 = (f32[4,24,768]{2,1,0:T(8,128)S(1)}, f32[4,24,768]{2,1,0:T(8,128)}, u32[]{:S(2)}) copy-start(f32[4,24,768]{2,1,0:T(8,128)} %param.22) | copy-start | bytes 884740
  7.2 30.5 %copy-start.4 = (f32[96,768]{1,0:T(8,128)S(1)}, f32[96,768]{1,0:T(8,128)}, u32[]{:S(2)}) copy-start(f32[96,768]{1,0:T(8,128)} %param.24) | copy-start | bytes 884740
  7.2 30.5 %copy-start.6 = (f32[768,64]{0,1:T(8,128)S(1)}, f32[768,64]{0,1:T(8,128)}, u32[]{:S(2)}) copy-start(f32[768,64]{0,1:T(8,128)} %param.35) | copy-start | bytes 589828
  7.2 28.1 %copy-start.3 = (f32[24,3072]{1,0:T(8,128)S(1)}, f32[24,3072]{1,0:T(8,128)}, u32[]{:S(2)}) copy-start(f32[24,3072]{1,0:T(8,128)} %param.23) | copy-start | bytes 884740
  7.2 28.1 %copy-start.1 = (f32[3072,64]{0,1:T(8,128)S(1)}, f32[3072,64]{0,1:T(8,128)}, u32[]{:S(2)}) copy-start(f32[3072,64]{0,1:T(8,128)} %param.34) | copy-start | bytes 2359300
  7.3 78.9 %all-gather.5.cloned.1.call-start = ((), (), s32[]{:S(2)}) async-start(), calls=%async_computation | async-start | bytes 4866048 | tf_op jit(solution)/shard_map/all_gather | solution.py:65
  8.7 63.3 %copy-start.9 = (f32[1,96,768]{2,1,0:T(8,128)S(1)}, f32[1,96,768]{2,1,0:T(8,128)}, u32[]{:S(2)}) copy-start(f32[1,96,768]{2,1,0:T(8,128)} %param.28) | copy-start | bytes 884740
  11.2 62.9 %copy-start.7 = (f32[1,24,3072]{2,1,0:T(8,128)S(1)}, f32[1,24,3072]{2,1,0:T(8,128)}, u32[]{:S(2)}) copy-start(f32[1,24,3072]{2,1,0:T(8,128)} %param.27) | copy-start | bytes 884740
  11.2 62.9 %copy-start.8 = (f32[1,24,3072]{2,1,0:T(8,128)S(1)}, f32[1,24,3072]{2,1,0:T(8,128)}, u32[]{:S(2)}) copy-start(f32[1,24,3072]{2,1,0:T(8,128)} %param.19) | copy-start | bytes 884740
  33.0 7.0 %copy-start.10 = (f32[4,24]{1,0:T(4,128)S(1)}, f32[4,24]{1,0:T(4,128)}, u32[]{:S(2)}) copy-start(f32[4,24]{1,0:T(4,128)} %get-tuple-element.14) | copy-start | bytes 1156
  35.3 99.8 %all-gather.7.cloned.1.call-start = ((), (), s32[]{:S(2)}) async-start(), calls=%async_computation.1 | async-start | bytes 4866048 | tf_op jit(solution)/shard_map/all_gather | solution.py:66
  37.6 146.5 %all-gather.9.cloned.1.call-start = ((), (), s32[]{:S(2)}) async-start(), calls=%async_computation.2 | async-start | bytes 4866048 | tf_op jit(solution)/shard_map/all_gather | solution.py:67
  184.1 5.2 %copy-start.2 = (bf16[768,3072]{1,0:T(8,128)(2,1)S(1)}, bf16[768,3072]{1,0:T(8,128)(2,1)}, u32[]{:S(2)}) copy-start(bf16[768,3072]{1,0:T(8,128)(2,1)} %all-gather.7.cloned.1.call-done) | copy-start | bytes 14155780
  184.1 8.0 %slice-start = ((s8[4718592]{0:T(1024)(128)(4,1)}), s8[4194304]{0:T(1024)(128)(4,1)S(1)}, s32[]{:S(2)}) async-start(s8[4718592]{0:T(1024)(128)(4,1)} %bitcast.63), calls=%async_computation.3 | async-start | bytes 8388608
  189.3 3.4 %slice-start.1 = ((s8[4718592]{0:T(1024)(128)(4,1)}), s8[524288]{0:T(1024)(128)(4,1)S(1)}, s32[]{:S(2)}) async-start(s8[4718592]{0:T(1024)(128)(4,1)} %bitcast.63), calls=%async_computation.4 | async-start | bytes 1048576
Sparse Core Ops, SparseCore 0:
  35.4 50.7 all-gather.4
  89.0 46.0 all-gather.6
  137.9 46.1 all-gather.8
where the time goes:
time: 202 us; the launch traced here: 201 us
  waiting for transfers between devices  106 us (52%)
  blocking collectives  46 us (23%)
  matrix products  19.4 us (10%)
  between operations  13.9 us (7%)
  local copies, waits for them, and re-layouts  13.4 us (7%)
  other arithmetic  2.13 us (1%)
    all_gather x1, waiting for transfers between devices, on_device(): lax.all_gather(owned_down, 'shard', axis=0, tiled=True)  49 us
    all_gather x1, waiting for transfers between devices, on_device(): lax.all_gather(owned_up, 'shard', axis=0, tiled=True)  49 us
    all_gather x1, blocking collectives, on_device(): lax.all_gather(norm_weights, 'shard', axis=1, tiled=True)  28.7 us
    psum x1, blocking collectives, on_device(): summed = lax.psum((factor_sq, factor_up, factor_down, norm_delta), 'rep')  17.3 us
    unnamed x30, local copies, waits for them, and re-layouts  12.8 us
    all_gather x1, waiting for transfers between devices, on_device(): lax.all_gather(owned_sq, 'shard', axis=1, tiled=True)  8.47 us
  transfers between devices with their start and end apart: 3, of which 3 were waited for; matrix products, arithmetic and copies ran while one was open for 7% of the time, Pallas kernels for 0%

commit v1 on v0

--- a/solution.py
+++ b/solution.py
@@ -5,6 +5,14 @@
 
 moment_coef = 0.9
 outer_rate = 0.7
+
+
+def gather_by_exchange(array, axis, dim):
+    size = lax.axis_size(axis)
+    repeats = [size if d == dim else 1 for d in range(array.ndim)]
+    return lax.all_to_all(
+        jnp.tile(array, repeats), axis, split_axis=dim, concat_axis=dim, tiled=True
+    )
 
 
 def advance(start, moment, outer):
@@ -63,7 +71,7 @@
     new_mom_down, owned_down = advance(start_down, mom_down, outer_down)
     weights_sq, weights_up, weights_down, weights_ln = (
         lax.all_gather(owned_sq, "shard", axis=1, tiled=True),
-        lax.all_gather(owned_up, "shard", axis=0, tiled=True),
+        gather_by_exchange(owned_up, "shard", 0),
         lax.all_gather(owned_down, "shard", axis=0, tiled=True),
         lax.all_gather(norm_weights, "shard", axis=1, tiled=True),
     )

time: 202 us -> 189 us (0.936)
  waiting for transfers between devices: 106 us -> 28.1 us
  blocking collectives: 46 us -> 99.4 us
  starting transfers between devices: 0.12 us -> 11.8 us
  local copies, waits for them, and re-layouts: 13.4 us -> 17.3 us
  matrix products: 19.4 us -> 16 us
    all_gather x1, blocking collectives: 28.7 us -> 82.6 us  [on_device(): lax.all_gather(norm_weights, 'shard', axis=1, tiled=True)]
    all_gather x1 -> x0, waiting for transfers between devices: 49 us -> none  [on_device(): lax.all_gather(owned_up, 'shard', axis=0, tiled=True)]
    all_gather x1, waiting for transfers between devices: 49 us -> 28.1 us  [on_device(): lax.all_gather(owned_down, 'shard', axis=0, tiled=True)]
    all_to_all x0 -> x1, starting transfers between devices: none -> 11.7 us  [gather_by_exchange(): lax.all_to_all(jnp.tile(array, repeats), axis, split_axis=dim, concat_axi...]
    all_gather x1, waiting for transfers between devices: 8.47 us -> 0.01 us  [on_device(): lax.all_gather(owned_sq, 'shard', axis=1, tiled=True)]
    another operation x0 -> x1, local copies, waits for them, and re-layouts: none -> 2.77 us  [gather_by_exchange(): jnp.tile(array, repeats)]
    unnamed x30 -> x36, local copies, waits for them, and re-layouts: 12.8 us -> 13.9 us
  transfers between devices with their start and end apart: 3 -> 3, of which waited for: 3 -> 1; matrix products, arithmetic and copies ran while one was open for 7% -> 8% of each run, Pallas kernels for 0% -> 0%
where the time goes in v1:
time: 189 us
  blocking collectives  99.4 us (53%)
  waiting for transfers between devices  28.1 us (15%)
  local copies, waits for them, and re-layouts  17.3 us (9%)
  matrix products  16 us (8%)
  between operations  14.2 us (8%)
  starting transfers between devices  11.8 us (6%)
  other arithmetic  2.13 us (1%)
    all_gather x1, blocking collectives, on_device(): lax.all_gather(norm_weights, 'shard', axis=1, tiled=True)  82.6 us
    all_gather x1, waiting for transfers between devices, on_device(): lax.all_gather(owned_down, 'shard', axis=0, tiled=True)  28.1 us
    psum x1, blocking collectives, on_device(): summed = lax.psum((factor_sq, factor_up, factor_down, norm_delta), 'rep')  16.8 us
    unnamed x36, local copies, waits for them, and re-layouts  13.9 us
    all_to_all x1, starting transfers between devices, gather_by_exchange(): lax.all_to_all(jnp.tile(array, repeats), axis, split_axis=dim, concat_axi...  11.7 us
  transfers between devices with their start and end apart: 3, of which 1 were waited for; matrix products, arithmetic and copies ran while one was open for 8% of the time, Pallas kernels for 0%

profile of v1, /device:TPU:1, one launch (start us, length us, event | category | flops | bytes accessed | tf_op | source)
XLA Modules:
  0.0 189.0 jit_solution(14513160146924526255)
XLA Ops:
  7.3 0.0 all-gather.4.cloned.1.call-start
  7.3 0.8 bitcast_subtract_fusion.3
  8.2 0.3 copy-done
  8.5 1.9 %fusion.16 = f32[4,24,64]{2,1,0:T(8,128)S(1)} fusion(f32[4,768,64]{1,2,0:T(8,128)S(1)} %copy-done, f32[1,4,24,768]{3,2,1,0:T(8,128)} %param.26, f32[4,24,768]{2,1,0:T(8,128)} %param.22, f32[1,4,24,768]{3,2,1,0:T(8,128)} %param.18), kind=kOutput, calls=%fused_computation.34 | convolution fusion | flops 56770560 | bytes 1695744 | tf_op jit(solution)/shard_map/mrd,mdk->mrk/dot_general | solution.py:47
  10.4 1.6 fusion.18
  12.0 2.1 %fusion.17 = f32[24,64]{1,0:T(8,128)S(1)} fusion(f32[3072,64]{0,1:T(8,128)} %param.34, f32[1,24,3072]{2,1,0:T(8,128)} %param.27, f32[24,3072]{1,0:T(8,128)} %param.23, f32[1,24,3072]{2,1,0:T(8,128)} %param.19), kind=kOutput, calls=%fused_computation.35 | convolution fusion | flops 56770560 | bytes 1677312 | tf_op jit(solution)/shard_map/dot_general | solution.py:50
  14.2 16.8 %all-reduce = (f32[4,24,64]{2,1,0:T(8,128)S(1)}, f32[24,64]{1,0:T(8,128)S(1)}, f32[96,64]{0,1:T(8,128)S(1)}, f32[4,24]{1,0:T(4,128)}) all-reduce(f32[4,24,64]{2,1,0:T(8,128)S(1)} %fusion.16, f32[24,64]{1,0:T(8,128)S(1)} %fusion.17, f32[96,64]{0,1:T(8,128)S(1)} %fusion.18, ...), channel_id=1, replica_groups=mesh['rep'=4,'shard'=32] {'rep'}, use_global_device_ids=true, to_apply=%region_0.0 | all-reduce | flops 13920 | bytes 111360 | tf_op jit(solution)/shard_map/psum | solution.py:60
  31.0 1.3 subtract_convert_fusion.2
  32.3 0.0 all-gather.6.cloned.1.call-start
  32.4 1.2 subtract_convert_fusion
  33.7 2.2 %subtract_convert_fusion.1 = (bf16[24,3072]{1,0:T(8,128)(2,1)S(1)}, f32[24,3072]{1,0:T(8,128)}) fusion(f32[24,3072]{1,0:T(8,128)S(1)} %copy-done.2, f32[24,3072]{1,0:T(8,128)} %param.30, f32[3072,64]{0,1:T(8,128)S(1)} %copy-done.1, f32[24,64]{1,0:T(8,128)S(1)} %get-tuple-element.12), kind=kOutput, calls=%fused_computation.13 | convolution fusion | flops 57140736 | bytes 1824768 | tf_op jit(solution)/shard_map/rk,fk->rf/dot_general | solution.py:67
  35.9 2.8 %tile.2 = bf16[32,24,3072]{2,1,0:T(8,128)(2,1)} broadcast(bf16[24,3072]{1,0:T(8,128)(2,1)S(1)} %get-tuple-element.19), dimensions={1,2} | broadcast | bytes 4866048 | tf_op jit(solution)/shard_map/tile | solution.py:14
  38.7 11.7 %all-to-all-start = ((bf16[32,24,3072]{2,1,0:T(8,128)(2,1)}), bf16[32,24,3072]{2,1,0:T(8,128)(2,1)}, u32[]{:S(2)}, u32[]{:S(2)}) async-start(bf16[32,24,3072]{2,1,0:T(8,128)(2,1)} %tile.2), calls=%async_computation | async-start | bytes 9437184 | tf_op jit(solution)/shard_map/all_to_all | solution.py:13
  50.4 1.3 fusion.12
  51.7 82.6 %all-gather = bf16[32,24,4]{1,2,0:T(4,128)(2,1)S(1)} all-gather(bf16[1,24,4]{1,2,0:T(4,128)(2,1)S(1)} %get-tuple-element.15), channel_id=1, replica_groups=mesh['rep'=4,'shard'=32] {'shard'}, dimensions={0}, use_global_device_ids=true | all-gather | bytes 6336 | tf_op jit(solution)/shard_map/all_gather | solution.py:76
  134.2 0.6 copy.30
  134.9 1.5 reshape.30
  136.3 2.1 %fusion.1 = f32[1,96,768]{2,1,0:T(8,128)} fusion(f32[96,64]{0,1:T(8,128)} %copy-done.12, f32[768,64]{0,1:T(8,128)S(1)} %copy-done.5, f32[1,96,768]{2,1,0:T(8,128)S(1)} %copy-done.8, f32[96,768]{1,0:T(8,128)S(1)} %copy-done.3, f32[1,96,768]{2,1,0:T(8,128)} %param.20), kind=kOutput, calls=%fused_computation.3 | convolution fusion | flops 56844288 | bytes 1400832 | tf_op jit(solution)/shard_map/rk,dk->rd/dot_general | solution.py:56
  138.5 1.2 fusion
  139.7 2.3 %fusion.2 = f32[1,4,24,768]{3,2,1,0:T(8,128)} fusion(f32[4,24,64]{2,1,0:T(8,128)} %copy-done.9, f32[4,768,64]{1,2,0:T(8,128)S(1)} %copy-done, f32[1,4,24,768]{3,2,1,0:T(8,128)} %param.26, f32[4,24,768]{2,1,0:T(8,128)S(1)} %copy-done.4, f32[1,4,24,768]{3,2,1,0:T(8,128)} %param.18), kind=kOutput, calls=%fused_computation.5 | convolution fusion | flops 56844288 | bytes 1990656 | tf_op jit(solution)/shard_map/mrk,mdk->mrd/dot_general | solution.py:48
  142.0 28.1 %all-gather.6.cloned.1.call-done = bf16[3072,768]{1,0:T(8,128)(2,1)} async-done(((bf16[96,768]{1,0:T(8,128)(2,1)}), bf16[3072,768]{1,0:T(8,128)(2,1)}) %all-gather.6.cloned.1.call-update) | async-done | bytes 4718608 | tf_op jit(solution)/shard_map/all_gather | solution.py:75
  170.1 5.0 %copy.34 = bf16[4,768,768]{2,1,0:T(8,128)(2,1)} copy(bf16[4,768,768]{2,1,0:T(8,128)(2,1)} %all-gather.4.cloned.1.call-done) | data formatting | bytes 9437184
  175.0 4.9 %copy.35 = bf16[768,3072]{1,0:T(8,128)(2,1)} copy(bf16[768,3072]{1,0:T(8,128)(2,1)} %bitcast.10) | data formatting | bytes 9437184
  179.9 2.2 %copy.36 = bf16[3072,768]{1,0:T(8,128)(2,1)} copy(bf16[3072,768]{1,0:T(8,128)(2,1)S(1)} %bitcast.65) | data formatting | bytes 9437184
  (36 shorter events, 0.1 us)
Async XLA Ops:
  7.2 1.3 copy-start
  7.2 23.8 %copy-start.4 = (f32[4,24,768]{2,1,0:T(8,128)S(1)}, f32[4,24,768]{2,1,0:T(8,128)}, u32[]{:S(2)}) copy-start(f32[4,24,768]{2,1,0:T(8,128)} %param.22) | copy-start | bytes 884740
  7.2 25.2 %copy-start.3 = (f32[96,768]{1,0:T(8,128)S(1)}, f32[96,768]{1,0:T(8,128)}, u32[]{:S(2)}) copy-start(f32[96,768]{1,0:T(8,128)} %param.24) | copy-start | bytes 884740
  7.2 25.2 %copy-start.5 = (f32[768,64]{0,1:T(8,128)S(1)}, f32[768,64]{0,1:T(8,128)}, u32[]{:S(2)}) copy-start(f32[768,64]{0,1:T(8,128)} %param.35) | copy-start | bytes 589828
  7.2 26.4 %copy-start.2 = (f32[24,3072]{1,0:T(8,128)S(1)}, f32[24,3072]{1,0:T(8,128)}, u32[]{:S(2)}) copy-start(f32[24,3072]{1,0:T(8,128)} %param.23) | copy-start | bytes 884740
  7.2 26.4 %copy-start.1 = (f32[3072,64]{0,1:T(8,128)S(1)}, f32[3072,64]{0,1:T(8,128)}, u32[]{:S(2)}) copy-start(f32[3072,64]{0,1:T(8,128)} %param.34) | copy-start | bytes 2359300
  7.3 23.7 %copy-start.10 = (f32[4,24,768]{2,1,0:T(8,128)S(1)}, f32[4,24,768]{2,1,0:T(8,128)}, u32[]{:S(2)}) copy-start(f32[4,24,768]{2,1,0:T(8,128)} %param.29) | copy-start | bytes 884740
  7.3 25.1 %copy-start.11 = (f32[96,768]{1,0:T(8,128)S(1)}, f32[96,768]{1,0:T(8,128)}, u32[]{:S(2)}) copy-start(f32[96,768]{1,0:T(8,128)} %param.31) | copy-start | bytes 884740
  7.3 134.7 %all-gather.4.cloned.1.call-start = ((), (), s32[]{:S(2)}) async-start(), calls=%async_computation.1 | async-start | bytes 4866048 | tf_op jit(solution)/shard_map/all_gather | solution.py:73
  10.4 25.5 %copy-start.9 = (f32[4,24,64]{2,1,0:T(8,128)}, f32[4,24,64]{2,1,0:T(8,128)S(1)}, u32[]{:S(2)}) copy-start(f32[4,24,64]{2,1,0:T(8,128)S(1)} %fusion.16) | copy-start | bytes 73732
  12.0 23.9 %copy-start.12 = (f32[96,64]{0,1:T(8,128)}, f32[96,64]{0,1:T(8,128)S(1)}, u32[]{:S(2)}) copy-start(f32[96,64]{0,1:T(8,128)S(1)} %fusion.18) | copy-start | bytes 73732
  32.3 137.7 %all-gather.6.cloned.1.call-start = ((), (), s32[]{:S(2)}) async-start(), calls=%async_computation.2 | async-start | bytes 4866048 | tf_op jit(solution)/shard_map/all_gather | solution.py:75
  38.7 11.7 %copy-start.13 = (f32[4,24]{1,0:T(4,128)S(1)}, f32[4,24]{1,0:T(4,128)}, u32[]{:S(2)}) copy-start(f32[4,24]{1,0:T(4,128)} %param.25) | copy-start | bytes 1156
  38.7 97.7 %copy-start.8 = (f32[1,96,768]{2,1,0:T(8,128)S(1)}, f32[1,96,768]{2,1,0:T(8,128)}, u32[]{:S(2)}) copy-start(f32[1,96,768]{2,1,0:T(8,128)} %param.28) | copy-start | bytes 884740
  38.7 99.8 %copy-start.6 = (f32[1,24,3072]{2,1,0:T(8,128)S(1)}, f32[1,24,3072]{2,1,0:T(8,128)}, u32[]{:S(2)}) copy-start(f32[1,24,3072]{2,1,0:T(8,128)} %param.27) | copy-start | bytes 884740
  38.7 99.8 %copy-start.7 = (f32[1,24,3072]{2,1,0:T(8,128)S(1)}, f32[1,24,3072]{2,1,0:T(8,128)}, u32[]{:S(2)}) copy-start(f32[1,24,3072]{2,1,0:T(8,128)} %param.19) | copy-start | bytes 884740
  38.7 103.3 %all-to-all-start = ((bf16[32,24,3072]{2,1,0:T(8,128)(2,1)}), bf16[32,24,3072]{2,1,0:T(8,128)(2,1)}, u32[]{:S(2)}, u32[]{:S(2)}) async-start(bf16[32,24,3072]{2,1,0:T(8,128)(2,1)} %tile.2), calls=%async_computation | async-start | bytes 9437184 | tf_op jit(solution)/shard_map/all_to_all | solution.py:13
  170.1 9.9 %slice-start = ((s8[4718592]{0:T(1024)(128)(4,1)}), s8[4194304]{0:T(1024)(128)(4,1)S(1)}, s32[]{:S(2)}) async-start(s8[4718592]{0:T(1024)(128)(4,1)} %bitcast.64), calls=%async_computation.3 | async-start | bytes 8388608
  175.0 4.9 %slice-start.1 = ((s8[4718592]{0:T(1024)(128)(4,1)}), s8[524288]{0:T(1024)(128)(4,1)S(1)}, s32[]{:S(2)}) async-start(s8[4718592]{0:T(1024)(128)(4,1)} %bitcast.64), calls=%async_computation.4 | async-start | bytes 1048576
Sparse Core Ops, SparseCore 0:
  32.4 88.8 all-gather.3
  124.1 45.8 all-gather.5
